TPU v7x, 256 devices: a whole 4x4x8 slice. The times are simulated.
256 devices in a mesh: row: 8 (over z_lo, y), col: 32 (over z_hi, x, core).
Axes of the slice: x: 4, y: 4, z: 8 (z_hi: 4, z_lo: 2; z = z_hi * 2 + z_lo), core: 2. Of those that a mesh axis runs over, the one named last changes fastest.
Arguments:
- strip: float32 [12, 2048, 2, 1024], P(None, 'col', None, 'row'), may hold values from -6 to 6
- lower: float32 [12, 2048, 2, 1024], P(None, 'col', None, 'row'), may hold values from -1.6 to 1.6, as said below
Outputs:
- reduced: float32 [12, 2048, 2, 1024], P(None, 'col', None, 'row')
Inputs may be any that keep to these rules, and one draw needn't show every extreme that they name: `lower`: in the first 2048 rows the diagonal lies between 0.8 and 1.6 and entries above it are zero.
All inputs are finite; a program needn't handle non-finite values.
Results may differ from a plain program's by a relative error of at most 0.00013.
Values sent between devices are 32-bit elements; how exact they have to be, the bound alone decides.
No kernel may reach another device: no remote copies, remote signals or barrier semaphores. Data moves between devices by JAX's collectives and lax.ppermute only.
A program may use at most 64 MiB of HBM per device.

v0:
```python
import jax
import jax.numpy as jnp
from jax import lax
from jax.sharding import PartitionSpec as P

highest = lax.Precision.HIGHEST


def times_rows(coeff, right_side):
    return jnp.dot(coeff, right_side, precision=highest, preferred_element_type=jnp.float32)


def times_rows_turned(coeff, right_turned):
    return lax.dot_general(
        coeff,
        right_turned,
        (((1,), (1,)), ((), ())),
        precision=highest,
        preferred_element_type=jnp.float32,
    )


def local(strip, lower):
    rounds = strip.shape[0]
    strip_width = strip.shape[1]
    row_run = strip.shape[3]
    row_count = lax.axis_size("row")
    col_count = lax.axis_size("col")
    block_size = row_run * row_count
    cols_here = rounds * strip_width
    trail_count = cols_here - strip_width
    share = block_size // col_count
    local_strip = strip.reshape(cols_here, 2, row_run)
    left_part = local_strip[:, 0, :]
    right_part = local_strip[:, 1, :]
    gathered = lax.all_gather(lower[0], "col", axis=0, tiled=True)
    first_cols = gathered[:block_size, 0, :]
    cross_cols = gathered[block_size:, 0, :]
    second_cols = gathered[block_size:, 1, :]
    col_position = lax.axis_index("col")
    start = col_position * share
    top_rows = lax.dynamic_slice_in_dim(gathered, start, share, 0)
    bottom_rows = lax.dynamic_slice_in_dim(gathered, block_size + start, share, 0)
    picked = jnp.concatenate([top_rows, bottom_rows], axis=0)
    picked_rows = lax.all_gather(picked, "row", axis=2, tiled=True)
    first_rows = picked_rows[:share, 0, :]
    cross_rows = picked_rows[share:, 0, :]
    second_rows = picked_rows[share:, 1, :]
    upper_half = lax.psum_scatter(
        times_rows_turned(first_cols, left_part), "row", scatter_dimension=0, tiled=True
    )
    carried = lax.psum_scatter(
        times_rows(cross_cols, upper_half), "row", scatter_dimension=0, tiled=True
    )
    remainder = right_part.T - carried
    lower_half = lax.psum_scatter(
        times_rows(second_cols, remainder), "row", scatter_dimension=0, tiled=True
    )
    solved = jnp.stack([upper_half.T, lower_half.T], axis=1)
    lead_rows = solved[:strip_width]
    tail_rows = solved[strip_width:].reshape(trail_count, 2 * row_run)
    lead_all = lax.all_gather(lead_rows, "col", axis=0, tiled=True)
    lead_all = lead_all.reshape(2 * block_size, 2 * row_run)
    first_piece = times_rows(first_rows, lead_all[:block_size])
    first_block = lax.all_gather(first_piece, "col", axis=0, tiled=True)
    lead_second = lax.dynamic_slice_in_dim(lead_all, block_size + start, share, 0)
    diff_piece = lead_second - times_rows(cross_rows, first_block)
    diff_block = lax.all_gather(diff_piece, "col", axis=0, tiled=True)
    second_piece = times_rows(second_rows, diff_block)
    second_block = lax.all_gather(second_piece, "col", axis=0, tiled=True)
    everything = jnp.concatenate([first_block, second_block], axis=0)
    solved_lead = lax.dynamic_slice_in_dim(everything, col_position * strip_width, strip_width, 0)
    left_rows = lower[1:].reshape(trail_count, 2 * row_run)
    grouped = everything.reshape(2, row_count, row_run, 2 * row_run).transpose(1, 0, 2, 3)
    swapped = lax.all_to_all(grouped, "row", split_axis=0, concat_axis=0, tiled=True)
    turned_block = swapped.reshape(row_count, 2, row_run, 2, row_run).transpose(0, 3, 4, 1, 2)
    turned_block = turned_block.reshape(row_count * 2 * row_run, 2 * row_run)
    summed = lax.psum_scatter(
        times_rows_turned(turned_block, left_rows), "row", scatter_dimension=0, tiled=True
    )
    update = summed.T
    reduced = jnp.concatenate([solved_lead, tail_rows - update], axis=0)
    return reduced.reshape(rounds, strip_width, 2, row_run)


def solution(mesh):
    in_specs = (P(None, "col", None, "row"), P(None, "col", None, "row"))
    out_specs = P(None, "col", None, "row")
    return jax.shard_map(local, mesh=mesh, in_specs=in_specs, out_specs=out_specs, check_vma=False)
```

profile of v0, /device:TPU:1, one launch (start us, length us, event | category | flops | bytes accessed | tf_op | source)
XLA Modules:
  0.0 562.7 jit_solution(11136738738206330280)
XLA Ops:
  6.5 1.5 slice_bitcast_fusion.3
  8.1 1.2 copy.9
  9.3 59.5 %all-gather.15.cloned.1.call-done = f32[1,2048,2,128]{3,2,0,1:T(2,128)} async-done(((f32[1,64,2,128]{3,2,0,1:T(2,128)}), f32[1,2048,2,128]{3,2,0,1:T(2,128)}) %all-gather.15.cloned.1.call-update) | async-done | bytes 2097168 | tf_op jit(solution)/shard_map/all_gather | solution.py:36
  68.8 3.2 fusion.18
  72.1 4.3 fusion.10
  76.4 41.6 %reduce-scatter.5.cloned.1.call-done = f32[128,768]{1,0:T(8,128)} async-done(((f32[1024,768]{1,0:T(8,128)}), f32[128,768]{1,0:T(8,128)}) %reduce-scatter.5.cloned.1.call-update) | async-done | bytes 393232 | tf_op jit(solution)/shard_map/reduce_scatter | solution.py:49
  118.0 5.3 convolution_bitcast_fusion.1
  123.4 48.2 %reduce-scatter.7.cloned.1.call-done = f32[128,768]{0,1:T(8,128)} async-done(((f32[1024,768]{0,1:T(8,128)}), f32[128,768]{0,1:T(8,128)}) %reduce-scatter.7.cloned.1.call-update) | async-done | bytes 393232 | tf_op jit(solution)/shard_map/reduce_scatter | solution.py:52
  171.6 5.3 convolution_bitcast_fusion
  177.0 48.3 %reduce-scatter.9.cloned.1.call-done = f32[128,768]{1,0:T(8,128)} async-done(((f32[1024,768]{1,0:T(8,128)}), f32[128,768]{1,0:T(8,128)}) %reduce-scatter.9.cloned.1.call-update) | async-done | bytes 393232 | tf_op jit(solution)/shard_map/reduce_scatter | solution.py:56
  227.7 16.4 %all_gather.19 = f32[64,2,1024]{2,1,0:T(2,128)S(1)} all-gather(f32[64,2,128]{2,1,0:T(2,128)S(1)} %pad_maximum_fusion.3), channel_id=1, replica_groups=mesh['row'=8,'col'=32] {'row'}, dimensions={2}, use_global_device_ids=true | all-gather | bytes 589824 | tf_op jit(solution)/shard_map/all_gather | solution.py:45
  244.1 1.0 fusion.19
  245.1 41.1 %all-gather.7.cloned.1.call-done = f32[2048,2,128]{2,1,0:T(2,128)} async-done(((f32[64,2,128]{2,1,0:T(2,128)}), f32[2048,2,128]{2,1,0:T(2,128)}) %all-gather.7.cloned.1.call-update) | async-done | bytes 2097168 | tf_op jit(solution)/shard_map/all_gather | solution.py:62
  286.2 1.2 slice-done
  287.4 2.1 fusion.3
  289.8 1.5 copy.51
  291.3 47.4 %all-gather.9.cloned.1.call-done = f32[1024,256]{1,0:T(8,128)} async-done(((f32[32,256]{1,0:T(8,128)}), f32[1024,256]{1,0:T(8,128)}) %all-gather.9.cloned.1.call-update) | async-done | bytes 1048592 | tf_op jit(solution)/shard_map/all_gather | solution.py:65
  338.7 2.5 convolution_subtract_fusion
  341.3 49.6 %all-gather.11.cloned.1.call-done = f32[1024,256]{1,0:T(8,128)} async-done(((f32[32,256]{1,0:T(8,128)}), f32[1024,256]{1,0:T(8,128)}) %all-gather.11.cloned.1.call-update) | async-done | bytes 1048592 | tf_op jit(solution)/shard_map/all_gather | solution.py:68
  390.9 2.4 fusion.13
  393.4 49.5 %all-gather.13.cloned.1.call-done = f32[1024,256]{1,0:T(8,128)} async-done(((f32[32,256]{1,0:T(8,128)}), f32[1024,256]{1,0:T(8,128)}) %all-gather.13.cloned.1.call-update) | async-done | bytes 1048592 | tf_op jit(solution)/shard_map/all_gather | solution.py:70
  443.0 1.3 constant_dynamic-update-slice_fusion
  444.3 1.7 copy.52
  446.2 4.3 all-to-all-start
  450.7 26.2 %all-to-all-done = f32[8,2,128,256]{3,2,1,0:T(8,128)} async-done(((f32[8,2,128,256]{3,2,1,0:T(8,128)}), f32[8,2,128,256]{3,2,1,0:T(8,128)}, u32[]{:S(2)}, u32[]{:S(2)}) %all-to-all-start) | async-done | bytes 2097184 | tf_op jit(solution)/shard_map/all_to_all | solution.py:75
  476.8 2.8 copy.16
  479.7 6.7 %fusion = f32[2048,704]{0,1:T(8,128)} fusion(f32[256,8,2,128]{3,2,1,0:T(2,128)S(1)} %bitcast.74, f32[88,8,2,128]{3,2,1,0:T(2,128)S(1)} %bitcast.83), kind=kOutput, calls=%fused_computation | convolution fusion | flops 4429185024 | bytes 8585216 | tf_op jit(solution)/shard_map/dot_general | solution.py:14
  486.4 1.0 copy-done.4
  487.9 0.9 constant_dynamic-slice_fusion
  488.7 64.9 %reduce-scatter.11.cloned.1.call-done = f32[256,704]{0,1:T(8,128)} async-done(((f32[2048,704]{0,1:T(8,128)}), f32[256,704]{0,1:T(8,128)}) %reduce-scatter.11.cloned.1.call-update) | async-done | bytes 720912 | tf_op jit(solution)/shard_map/reduce_scatter | solution.py:78
  553.6 1.2 bitcast_subtract_fusion
  554.9 1.3 reshape.32
  (42 shorter events, 4.0 us)
Async XLA Ops:
  6.5 62.3 %all-gather.15.cloned.1.call-start = ((), (), s32[]{:S(2)}) async-start(), calls=%async_computation.13 | async-start | bytes 2162688 | tf_op jit(solution)/shard_map/all_gather | solution.py:36
  8.0 110.0 %reduce-scatter.5.cloned.1.call-start = ((), (), s32[]{:S(2)}) async-start(), calls=%async_computation.5 | async-start | bytes 3538944 | tf_op jit(solution)/shard_map/reduce_scatter | solution.py:49
  76.4 95.3 %reduce-scatter.7.cloned.1.call-start = ((), (), s32[]{:S(2)}) async-start(), calls=%async_computation.6 | async-start | bytes 3538944 | tf_op jit(solution)/shard_map/reduce_scatter | solution.py:52
  123.3 101.9 %reduce-scatter.9.cloned.1.call-start = ((), (), s32[]{:S(2)}) async-start(), calls=%async_computation.7 | async-start | bytes 3538944 | tf_op jit(solution)/shard_map/reduce_scatter | solution.py:56
  176.9 48.4 %copy-start.3 = (f32[128,768]{1,0:T(8,128)S(1)}, f32[128,768]{1,0:T(8,128)}, u32[]{:S(2)}) copy-start(f32[128,768]{1,0:T(8,128)} %reduce-scatter.5.cloned.1.call-done) | copy-start | bytes 1179652
  176.9 109.3 %all-gather.7.cloned.1.call-start = ((), (), s32[]{:S(2)}) async-start(), calls=%async_computation.8 | async-start | bytes 2162688 | tf_op jit(solution)/shard_map/all_gather | solution.py:62
  226.8 111.9 %all-gather.9.cloned.1.call-start = ((), (), s32[]{:S(2)}) async-start(), calls=%async_computation.9 | async-start | bytes 1081344 | tf_op jit(solution)/shard_map/all_gather | solution.py:65
  286.2 1.2 slice-start
  286.2 3.6 copy-start.1
  289.5 101.4 %all-gather.11.cloned.1.call-start = ((), (), s32[]{:S(2)}) async-start(), calls=%async_computation.10 | async-start | bytes 1081344 | tf_op jit(solution)/shard_map/all_gather | solution.py:68
  289.8 49.0 %copy-start.6 = (f32[32,1,1024]{2,1,0:T(1,128)S(1)}, f32[32,1,1024]{2,1,0:T(1,128)}, u32[]{:S(2)}) copy-start(f32[32,1,1024]{2,1,0:T(1,128)} %get-tuple-element.11) | copy-start | bytes 393220
  289.8 101.1 %copy-start.5 = (f32[32,1,1024]{2,1,0:T(1,128)S(1)}, f32[32,1,1024]{2,1,0:T(1,128)}, u32[]{:S(2)}) copy-start(f32[32,1,1024]{2,1,0:T(1,128)} %get-tuple-element.10) | copy-start | bytes 393220
  338.7 54.6 %copy-start.2 = (f32[1024,256]{1,0:T(8,128)S(1)}, f32[1024,256]{1,0:T(8,128)}, u32[]{:S(2)}) copy-start(f32[1024,256]{1,0:T(8,128)} %all-gather.9.cloned.1.call-done) | copy-start | bytes 3145732
  341.3 101.7 %all-gather.13.cloned.1.call-start = ((), (), s32[]{:S(2)}) async-start(), calls=%async_computation.11 | async-start | bytes 1081344 | tf_op jit(solution)/shard_map/all_gather | solution.py:70
  444.3 2.0 copy-start
  446.2 30.6 %all-to-all-start = ((f32[8,2,128,256]{3,2,1,0:T(8,128)}), f32[8,2,128,256]{3,2,1,0:T(8,128)}, u32[]{:S(2)}, u32[]{:S(2)}) async-start(f32[8,2,128,256]{3,2,1,0:T(8,128)} %bitcast.73), calls=%async_computation.3 | async-start | bytes 4194304 | tf_op jit(solution)/shard_map/all_to_all | solution.py:75
  450.6 103.0 %reduce-scatter.11.cloned.1.call-start = ((), (), s32[]{:S(2)}) async-start(), calls=%async_computation.12 | async-start | bytes 6488064 | tf_op jit(solution)/shard_map/reduce_scatter | solution.py:78
  450.6 29.0 %slice-start.1 = ((f32[12,64,2,128]{3,2,1,0:T(2,128)}), f32[11,64,2,128]{3,2,1,0:T(2,128)S(1)}, s32[]{:S(2)}) async-start(f32[12,64,2,128]{3,2,1,0:T(2,128)} %param.3), calls=%async_computation.15 | async-start | bytes 1441792 | tf_op jit(solution)/shard_map/slice | solution.py:73
  486.3 1.0 copy-start.4
Sparse Core Ops, SparseCore 0:
  9.9 58.8 all-gather.14
  76.5 41.5 reduce-scatter.4
  123.5 48.1 reduce-scatter.6
  177.0 48.1 reduce-scatter.8
  227.6 58.4 all-gather.6
  289.6 49.0 all-gather.8
  341.4 49.4 all-gather.10
  393.5 49.4 all-gather.12
  486.5 67.0 reduce-scatter.10
where the time goes:
time: 563 us
  waiting for transfers between devices  476 us (85%)
  matrix products  28.5 us (5%)
  local copies, waits for them, and re-layouts  20.7 us (4%)
  blocking collectives  16.4 us (3%)
  between operations  13.3 us (2%)
    reduce_scatter x1, waiting for transfers between devices, local(): lax.psum_scatter(times_rows_turned(turned_block, left_rows), 'row', scatt...  64.9 us
    all_gather x1, waiting for transfers between devices, local(): gathered = lax.all_gather(lower[0], 'col', axis=0, tiled=True)  59.5 us
    all_gather x1, waiting for transfers between devices, local(): diff_block = lax.all_gather(diff_piece, 'col', axis=0, tiled=True)  49.6 us
    all_gather x1, waiting for transfers between devices, local(): second_block = lax.all_gather(second_piece, 'col', axis=0, tiled=True)  49.5 us
    reduce_scatter x1, waiting for transfers between devices, local(): lax.psum_scatter(times_rows(second_cols, remainder), 'row', scatter_dimen...  48.3 us
    reduce_scatter x1, waiting for transfers between devices, local(): lax.psum_scatter(times_rows(cross_cols, upper_half), 'row', scatter_dimen...  48.2 us
    all_gather x1, waiting for transfers between devices, local(): first_block = lax.all_gather(first_piece, 'col', axis=0, tiled=True)  47.4 us
    reduce_scatter x1, waiting for transfers between devices, local(): lax.psum_scatter(times_rows_turned(first_cols, left_part), 'row', scatter...  41.6 us
  transfers between devices with their start and end apart: 10, of which 10 were waited for; matrix products, arithmetic and copies ran while one was open for 1% of the time, Pallas kernels for 0%

commit v1 on v0

--- a/solution.py
+++ b/solution.py
@@ -21,6 +21,12 @@
 
 
 def local(strip, lower):
+
+    def produce_quarters(in_array, lane_axis):
+        all_rows = jnp.stack(lax.axis_size(lane_axis) * [in_array], 0)
+        moved = lax.all_to_all(all_rows, lane_axis, 0, 0)
+        return jnp.concatenate(moved, axis=0)
+
     rounds = strip.shape[0]
     strip_width = strip.shape[1]
     row_run = strip.shape[3]
@@ -59,7 +65,7 @@
     solved = jnp.stack([upper_half.T, lower_half.T], axis=1)
     lead_rows = solved[:strip_width]
     tail_rows = solved[strip_width:].reshape(trail_count, 2 * row_run)
-    lead_all = lax.all_gather(lead_rows, "col", axis=0, tiled=True)
+    lead_all = produce_quarters(lead_rows, "col")
     lead_all = lead_all.reshape(2 * block_size, 2 * row_run)
     first_piece = times_rows(first_rows, lead_all[:block_size])
     first_block = lax.all_gather(first_piece, "col", axis=0, tiled=True)

time: 563 us -> 582 us (1.034)
  blocking collectives: 16.4 us -> 59 us
  waiting for transfers between devices: 476 us -> 440 us
  starting transfers between devices: 4.86 us -> 17.6 us
    all_gather x1, blocking collectives: 16.4 us -> 59 us  [local(): picked_rows = lax.all_gather(picked, 'row', axis=2, tiled=True)]
    all_gather x1 -> x0, waiting for transfers between devices: 41.1 us -> none  [local(): lead_all = lax.all_gather(lead_rows, 'col', axis=0, tiled=True)]
    all_to_all x0 -> x1, starting transfers between devices: none -> 13 us  [produce_quarters(): moved = lax.all_to_all(all_rows, lane_axis, 0, 0)]
  transfers between devices with their start and end apart: 10 -> 10, of which waited for: 10 -> 9; matrix products, arithmetic and copies ran while one was open for 1% -> 1% of each run, Pallas kernels for 0% -> 0%
where the time goes in v1:
time: 582 us; the launch traced here: 581 us
  waiting for transfers between devices  440 us (76%)
  blocking collectives  59 us (10%)
  matrix products  27.7 us (5%)
  local copies, waits for them, and re-layouts  21.1 us (4%)
  starting transfers between devices  17.6 us (3%)
  between operations  13.6 us (2%)
    reduce_scatter x1, waiting for transfers between devices, local(): lax.psum_scatter(times_rows_turned(turned_block, left_rows), 'row', scatt...  64.9 us
    all_gather x1, waiting for transfers between devices, local(): gathered = lax.all_gather(lower[0], 'col', axis=0, tiled=True)  59.5 us
    all_gather x1, blocking collectives, local(): picked_rows = lax.all_gather(picked, 'row', axis=2, tiled=True)  59 us
    all_gather x1, waiting for transfers between devices, local(): first_block = lax.all_gather(first_piece, 'col', axis=0, tiled=True)  51.9 us
    all_gather x1, waiting for transfers between devices, local(): diff_block = lax.all_gather(diff_piece, 'col', axis=0, tiled=True)  49.6 us
    all_gather x1, waiting for transfers between devices, local(): second_block = lax.all_gather(second_piece, 'col', axis=0, tiled=True)  49.5 us
    reduce_scatter x1, waiting for transfers between devices, local(): lax.psum_scatter(times_rows(second_cols, remainder), 'row', scatter_dimen...  48.5 us
    reduce_scatter x1, waiting for transfers between devices, local(): lax.psum_scatter(times_rows(cross_cols, upper_half), 'row', scatter_dimen...  48.4 us
  transfers between devices with their start and end apart: 10, of which 9 were waited for; matrix products, arithmetic and copies ran while one was open for 1% of the time, Pallas kernels for 0%

profile of v1, /device:TPU:1, one launch (start us, length us, event | category | flops | bytes accessed | tf_op | source)
XLA Modules:
  0.0 581.4 jit_solution(7855718678855229006)
XLA Ops:
  6.5 1.5 slice_bitcast_fusion.3
  8.1 1.2 copy.11
  9.3 59.5 %all-gather.12.cloned.1.call-done = f32[1,2048,2,128]{3,2,0,1:T(2,128)} async-done(((f32[1,64,2,128]{3,2,0,1:T(2,128)}), f32[1,2048,2,128]{3,2,0,1:T(2,128)}) %all-gather.12.cloned.1.call-update) | async-done | bytes 2097168 | tf_op jit(solution)/shard_map/all_gather | solution.py:42
  68.8 3.3 fusion.18
  72.1 4.2 fusion.10
  76.4 41.4 %reduce-scatter.5.cloned.1.call-done = f32[128,768]{1,0:T(8,128)} async-done(((f32[1024,768]{1,0:T(8,128)}), f32[128,768]{1,0:T(8,128)}) %reduce-scatter.5.cloned.1.call-update) | async-done | bytes 393232 | tf_op jit(solution)/shard_map/reduce_scatter | solution.py:55
  117.9 5.3 convolution_bitcast_fusion.1
  123.2 48.4 %reduce-scatter.7.cloned.1.call-done = f32[128,768]{0,1:T(8,128)} async-done(((f32[1024,768]{0,1:T(8,128)}), f32[128,768]{0,1:T(8,128)}) %reduce-scatter.7.cloned.1.call-update) | async-done | bytes 393232 | tf_op jit(solution)/shard_map/reduce_scatter | solution.py:58
  171.6 5.3 convolution_bitcast_fusion
  176.9 48.5 %reduce-scatter.9.cloned.1.call-done = f32[128,768]{1,0:T(8,128)} async-done(((f32[1024,768]{1,0:T(8,128)}), f32[128,768]{1,0:T(8,128)}) %reduce-scatter.9.cloned.1.call-update) | async-done | bytes 393232 | tf_op jit(solution)/shard_map/reduce_scatter | solution.py:62
  226.4 2.3 stack.11
  228.6 13.0 %all-to-all-start = ((f32[32,64,2,128]{3,2,1,0:T(2,128)}), f32[32,64,2,128]{3,2,1,0:T(2,128)S(1)}, u32[]{:S(2)}, u32[]{:S(2)}) async-start(f32[32,64,2,128]{3,2,1,0:T(2,128)} %stack.11), calls=%async_computation.3 | async-start | bytes 4194304 | tf_op jit(solution)/shard_map/all_to_all | solution.py:27
  242.5 59.0 %all_gather.16 = f32[64,2,1024]{2,1,0:T(2,128)S(1)} all-gather(f32[64,2,128]{2,1,0:T(2,128)S(1)} %pad_maximum_fusion.3), channel_id=1, replica_groups=mesh['row'=8,'col'=32] {'row'}, dimensions={2}, use_global_device_ids=true | all-gather | bytes 589824 | tf_op jit(solution)/shard_map/all_gather | solution.py:51
  301.5 1.0 fusion.19
  302.5 1.2 fusion.3
  303.8 1.5 copy.53
  305.3 51.9 %all-gather.6.cloned.1.call-done = f32[1024,256]{1,0:T(8,128)} async-done(((f32[32,256]{1,0:T(8,128)}), f32[1024,256]{1,0:T(8,128)}) %all-gather.6.cloned.1.call-update) | async-done | bytes 1048592 | tf_op jit(solution)/shard_map/all_gather | solution.py:71
  357.2 2.5 convolution_subtract_fusion
  359.7 49.6 %all-gather.8.cloned.1.call-done = f32[1024,256]{1,0:T(8,128)} async-done(((f32[32,256]{1,0:T(8,128)}), f32[1024,256]{1,0:T(8,128)}) %all-gather.8.cloned.1.call-update) | async-done | bytes 1048592 | tf_op jit(solution)/shard_map/all_gather | solution.py:74
  409.3 2.5 fusion.13
  411.9 49.5 %all-gather.10.cloned.1.call-done = f32[1024,256]{1,0:T(8,128)} async-done(((f32[32,256]{1,0:T(8,128)}), f32[1024,256]{1,0:T(8,128)}) %all-gather.10.cloned.1.call-update) | async-done | bytes 1048592 | tf_op jit(solution)/shard_map/all_gather | solution.py:76
  461.5 1.3 constant_dynamic-update-slice_fusion
  462.8 1.7 copy.54
  464.7 4.3 all-to-all-start.1
  469.1 26.2 %all-to-all-done.1 = f32[8,2,128,256]{3,2,1,0:T(8,128)} async-done(((f32[8,2,128,256]{3,2,1,0:T(8,128)}), f32[8,2,128,256]{3,2,1,0:T(8,128)}, u32[]{:S(2)}, u32[]{:S(2)}) %all-to-all-start.1) | async-done | bytes 2097184 | tf_op jit(solution)/shard_map/all_to_all | solution.py:81
  495.3 2.8 copy.18
  498.2 6.7 %fusion = f32[2048,704]{0,1:T(8,128)} fusion(f32[256,8,2,128]{3,2,1,0:T(2,128)S(1)} %bitcast.76, f32[88,8,2,128]{3,2,1,0:T(2,128)S(1)} %bitcast.85), kind=kOutput, calls=%fused_computation | convolution fusion | flops 4429185024 | bytes 8585216 | tf_op jit(solution)/shard_map/dot_general | solution.py:14
  504.8 1.0 copy-done.3
  506.3 0.9 constant_dynamic-slice_fusion
  507.2 64.9 %reduce-scatter.11.cloned.1.call-done = f32[256,704]{0,1:T(8,128)} async-done(((f32[2048,704]{0,1:T(8,128)}), f32[256,704]{0,1:T(8,128)}) %reduce-scatter.11.cloned.1.call-update) | async-done | bytes 720912 | tf_op jit(solution)/shard_map/reduce_scatter | solution.py:84
  572.1 1.2 bitcast_subtract_fusion
  573.3 1.3 reshape.30
  (35 shorter events, 3.2 us)
Async XLA Ops:
  6.5 62.3 %all-gather.12.cloned.1.call-start = ((), (), s32[]{:S(2)}) async-start(), calls=%async_computation.13 | async-start | bytes 2162688 | tf_op jit(solution)/shard_map/all_gather | solution.py:42
  8.0 109.8 %reduce-scatter.5.cloned.1.call-start = ((), (), s32[]{:S(2)}) async-start(), calls=%async_computation.6 | async-start | bytes 3538944 | tf_op jit(solution)/shard_map/reduce_scatter | solution.py:55
  76.4 95.2 %reduce-scatter.7.cloned.1.call-start = ((), (), s32[]{:S(2)}) async-start(), calls=%async_computation.7 | async-start | bytes 3538944 | tf_op jit(solution)/shard_map/reduce_scatter | solution.py:58
  123.2 102.2 %reduce-scatter.9.cloned.1.call-start = ((), (), s32[]{:S(2)}) async-start(), calls=%async_computation.8 | async-start | bytes 3538944 | tf_op jit(solution)/shard_map/reduce_scatter | solution.py:62
  176.9 48.6 %copy-start.2 = (f32[128,768]{1,0:T(8,128)S(1)}, f32[128,768]{1,0:T(8,128)}, u32[]{:S(2)}) copy-start(f32[128,768]{1,0:T(8,128)} %reduce-scatter.5.cloned.1.call-done) | copy-start | bytes 1179652
  228.6 73.8 %all-to-all-start = ((f32[32,64,2,128]{3,2,1,0:T(2,128)}), f32[32,64,2,128]{3,2,1,0:T(2,128)S(1)}, u32[]{:S(2)}, u32[]{:S(2)}) async-start(f32[32,64,2,128]{3,2,1,0:T(2,128)} %stack.11), calls=%async_computation.3 | async-start | bytes 4194304 | tf_op jit(solution)/shard_map/all_to_all | solution.py:27
  241.6 115.5 %all-gather.6.cloned.1.call-start = ((), (), s32[]{:S(2)}) async-start(), calls=%async_computation.9 | async-start | bytes 1081344 | tf_op jit(solution)/shard_map/all_gather | solution.py:71
  303.8 105.6 %all-gather.8.cloned.1.call-start = ((), (), s32[]{:S(2)}) async-start(), calls=%async_computation.10 | async-start | bytes 1081344 | tf_op jit(solution)/shard_map/all_gather | solution.py:74
  357.1 54.7 %copy-start.1 = (f32[1024,256]{1,0:T(8,128)S(1)}, f32[1024,256]{1,0:T(8,128)}, u32[]{:S(2)}) copy-start(f32[1024,256]{1,0:T(8,128)} %all-gather.6.cloned.1.call-done) | copy-start | bytes 3145732
  359.7 101.8 %all-gather.10.cloned.1.call-start = ((), (), s32[]{:S(2)}) async-start(), calls=%async_computation.11 | async-start | bytes 1081344 | tf_op jit(solution)/shard_map/all_gather | solution.py:76
  462.8 1.9 copy-start
  464.7 30.6 %all-to-all-start.1 = ((f32[8,2,128,256]{3,2,1,0:T(8,128)}), f32[8,2,128,256]{3,2,1,0:T(8,128)}, u32[]{:S(2)}, u32[]{:S(2)}) async-start(f32[8,2,128,256]{3,2,1,0:T(8,128)} %bitcast.75), calls=%async_computation.4 | async-start | bytes 4194304 | tf_op jit(solution)/shard_map/all_to_all | solution.py:81
  469.1 103.0 %reduce-scatter.11.cloned.1.call-start = ((), (), s32[]{:S(2)}) async-start(), calls=%async_computation.12 | async-start | bytes 6488064 | tf_op jit(solution)/shard_map/reduce_scatter | solution.py:84
  469.1 29.0 %slice-start = ((f32[12,64,2,128]{3,2,1,0:T(2,128)}), f32[11,64,2,128]{3,2,1,0:T(2,128)S(1)}, s32[]{:S(2)}) async-start(f32[12,64,2,128]{3,2,1,0:T(2,128)} %param.3), calls=%async_computation.14 | async-start | bytes 1441792 | tf_op jit(solution)/shard_map/slice | solution.py:79
  504.8 1.0 copy-start.3
Sparse Core Ops, SparseCore 0:
  9.9 58.8 all-gather.11
  76.5 41.3 reduce-scatter.4
  123.3 48.2 reduce-scatter.6
  177.0 48.3 reduce-scatter.8
  303.9 53.2 all-gather.5
  359.8 49.4 all-gather.7
  412.0 49.4 all-gather.9
  505.0 67.0 reduce-scatter.10
